TPU v7x, 256 devices: a whole 4x4x8 slice. The times are simulated.
256 devices in a mesh: pipe: 2 (over core), expert: 128 (over x, z, y).
Axes of the slice: x: 4, y: 4, z: 8, core: 2. Of those that a mesh axis runs over, the one named last changes fastest.
Arguments:
- section_inputs: bfloat16 [2, 16384, 7168], P('pipe', 'expert'), may hold values from -6 to 6
- output_grads: bfloat16 [2, 16384, 7168], P('pipe', 'expert'), may hold values from -6 to 6
- w_gate: bfloat16 [2, 7168, 16384], P('pipe', None, 'expert'), may hold values from -0.0625 to 0.0625
- w_up: bfloat16 [2, 7168, 16384], P('pipe', None, 'expert'), may hold values from -0.0625 to 0.0625
- w_down: bfloat16 [2, 16384, 7168], P('pipe', 'expert'), may hold values from -0.125 to 0.125
- route_ids: int32 [2, 16384, 8], P('pipe', 'expert'), may hold values from 0 to 255, all different within a row; in each aligned block of 128 rows (0 to 127, 128 to 255, ..., all dimensions but the last counted through in order) at most 5 rows name the same one
- route_gates: float32 [2, 16384, 8], P('pipe', 'expert'), may hold values from 0.25 to 1
Outputs:
- handed_grads: bfloat16 [2, 16384, 7168], P('pipe', 'expert')
- down_grads: bfloat16 [2, 16384, 7168], P('pipe', 'expert')
Inputs may be any that keep to these rules, and one draw needn't show every extreme that they name: `route_ids`: each row names 8 different experts. Within the 128 rows of one device of one section, no expert is named by more than 5 rows.
All inputs are finite; a program needn't handle non-finite values.
Results may differ from a plain program's by a relative error of at most 0.0057.
Values may be sent and summed in bfloat16 or wider, within the bound.
No kernel may reach another device: no remote copies, remote signals or barrier semaphores. Data moves between devices by JAX's collectives and lax.ppermute only.
A program may use at most 192 MiB of HBM per device.

v0:
```python
import jax
import jax.numpy as jnp
from jax import lax
from jax.sharding import Mesh
from jax.sharding import PartitionSpec as P

SHARDS = 16
CAP = 5
TILE_ROWS = 16


def from_behind(value, axis, steps):
    count = lax.axis_size(axis)
    pairs = [(source, (source + steps) % count) for source in range(count)]
    return lax.ppermute(value, axis, pairs)


def body(section_inputs, output_grads, w_gate, w_up, w_down, route_ids, route_gates):
    inputs = section_inputs[0]
    grads = output_grads[0]
    route = route_ids[0]
    gate = route_gates[0]
    gate_cols = w_gate[0]
    up_cols = w_up[0]
    down_rows = w_down[0]
    tok_rows, model_width = inputs.shape
    block_width = gate_cols.shape[1]
    live_count = lax.axis_size("group")
    slot_count = CAP
    expert_ids = jnp.arange(live_count, dtype=jnp.int32)
    hit = route[:, :, None] == expert_ids
    member = jnp.sum(hit.astype(jnp.int32), axis=1)
    weight = jnp.sum(jnp.where(hit, gate[:, :, None], 0.0), axis=1)
    position = jnp.cumsum(member, axis=0) - member
    slot_ids = jnp.arange(slot_count, dtype=jnp.int32)
    pick = (member[:, :, None] == 1) & (position[:, :, None] == slot_ids)
    pick_mat = pick.astype(jnp.bfloat16).reshape(tok_rows, live_count * slot_count)
    rows_first = (((0,), (0,)), ((), ()))
    rows_in = lax.dot_general(
        pick_mat, inputs, rows_first, preferred_element_type=jnp.float32
    ).astype(jnp.bfloat16)
    chosen_grads = lax.dot_general(pick_mat, grads, rows_first, preferred_element_type=jnp.float32)
    slot_gate = jnp.sum(pick.astype(jnp.float32) * weight[:, :, None], axis=0).reshape(
        live_count * slot_count, 1
    )
    rows_grad = (chosen_grads * slot_gate).astype(jnp.bfloat16)
    send_in = rows_in.reshape(live_count, TILE_ROWS, -1)
    send_grad = rows_grad.reshape(live_count, TILE_ROWS, -1)
    near_rows = live_count * slot_count
    near_in = lax.all_to_all(send_in, "group", 0, 0, tiled=True).reshape(near_rows, model_width)
    near_grad = lax.all_to_all(send_grad, "group", 0, 0, tiled=True).reshape(near_rows, model_width)
    got_in = lax.all_gather(near_in, "member", axis=0, tiled=True)
    got_grad = lax.all_gather(near_grad, "member", axis=0, tiled=True)
    both_cols = jnp.concatenate([gate_cols, up_cols], axis=1)
    both_cols, got_in, got_grad = lax.optimization_barrier((both_cols, got_in, got_grad))
    both_slice = lax.all_to_all(
        both_cols.reshape(SHARDS, -1, both_cols.shape[1]), "member", 0, 0, tiled=True
    )
    members = lax.axis_size("member")
    groups = live_count
    gate_pre = jnp.dot(got_in, gate_cols, preferred_element_type=jnp.float32)
    up_pre = jnp.dot(got_in, up_cols, preferred_element_type=jnp.float32)
    sigma = jax.nn.sigmoid(gate_pre)
    silu_gate = gate_pre * sigma
    hidden = (silu_gate * up_pre).astype(jnp.bfloat16)
    contract = (((1,), (1,)), ((), ()))
    back_hidden = lax.dot_general(got_grad, down_rows, contract, preferred_element_type=jnp.float32)
    grad_gate = (back_hidden * up_pre * sigma * (1.0 + gate_pre * (1.0 - sigma))).astype(
        jnp.bfloat16
    )
    grad_up = (back_hidden * silu_gate).astype(jnp.bfloat16)
    both_grad = jnp.concatenate([grad_gate, grad_up], axis=1).T
    down_part = lax.dot_general(
        hidden, got_grad, rows_first, preferred_element_type=jnp.float32
    ).astype(jnp.bfloat16)
    both_slice, both_grad, down_part = lax.optimization_barrier((both_slice, both_grad, down_part))
    all_grad = lax.all_gather(both_grad, "member", axis=0, tiled=False)
    slice_value = lax.dot_general(
        all_grad, both_slice, (((0, 1), (0, 2)), ((), ())), preferred_element_type=jnp.float32
    )
    slice_width = slice_value.shape[1]
    slice_value = slice_value.reshape(members, groups, slot_count, slice_width)
    slice_value = jnp.transpose(slice_value, (1, 0, 2, 3)).reshape(
        groups * members, slot_count, slice_width
    )
    back = lax.all_to_all(slice_value.astype(jnp.bfloat16), ("group", "member"), 0, 0, tiled=True)
    back = back.reshape(groups, members, slot_count, slice_width)
    returned = jnp.transpose(back, (0, 2, 1, 3)).reshape(groups * slot_count, model_width)
    other_grads = from_behind(grads, "pipe", -1)
    other_pick = from_behind(pick_mat, "pipe", -1)
    other_returned = from_behind(returned, "pipe", -1)
    branch = jnp.dot(other_pick, other_returned, preferred_element_type=jnp.float32)
    handed = (other_grads.astype(jnp.float32) + branch).astype(jnp.bfloat16)
    return (handed[None], down_part[None])


def solution(mesh):
    pipe = mesh.shape["pipe"]
    width = mesh.shape["expert"]
    groups = width // SHARDS
    inner = Mesh(mesh.devices.reshape(pipe, groups, SHARDS), ("pipe", "group", "member"))
    rows = P("pipe", ("group", "member"), None)
    cols = P("pipe", None, ("group", "member"))
    return jax.shard_map(
        body,
        mesh=inner,
        in_specs=(rows, rows, cols, cols, rows, rows, rows),
        out_specs=(rows, rows),
        check_vma=False,
    )
```

profile of v0, /device:TPU:1, one launch (start us, length us, event | category | flops | bytes accessed | tf_op | source)
XLA Modules:
  0.0 497.3 jit_solution(12213174864542856389)
XLA Ops:
  7.2 0.8 convert_reduce_fusion
  8.5 0.7 select_reduce_fusion.1
  9.3 1.9 fusion
  11.2 1.0 reshape.113
  12.2 26.1 %all_to_all.20 = bf16[8,16,2240]{2,1,0:T(8,128)(2,1)S(1)} all-to-all(bf16[8,16,2240]{2,1,0:T(8,128)(2,1)S(1)} %reshape.113), channel_id=1, replica_groups=mesh['pipe'=2,'group'=8,'member'=16] {'group'}, dimensions={0} | all-to-all | bytes 1146880 | tf_op jit(solution)/shard_map/all_to_all | solution.py:51
  38.3 1.7 reshape.114
  40.1 0.4 convolution_convert_fusion.1
  40.5 1.0 reshape.111
  41.5 14.6 %all_to_all.21 = bf16[8,16,2240]{2,1,0:T(8,128)(2,1)S(1)} all-to-all(bf16[8,16,2240]{2,1,0:T(8,128)(2,1)S(1)} %reshape.111), channel_id=1, replica_groups=mesh['pipe'=2,'group'=8,'member'=16] {'group'}, dimensions={0} | all-to-all | bytes 1146880 | tf_op jit(solution)/shard_map/all_to_all | solution.py:50
  56.1 1.7 reshape.112
  57.9 4.3 pad_maximum_fusion
  62.2 96.5 %all-gather.7.cloned.1.call-done = bf16[640,7168]{1,0:T(8,128)(2,1)} async-done(((bf16[40,7168]{1,0:T(8,128)(2,1)}), bf16[640,7168]{1,0:T(8,128)(2,1)}) %all-gather.7.cloned.1.call-update) | async-done | bytes 9175056 | tf_op jit(solution)/shard_map/all_gather | solution.py:53
  158.7 109.4 %all-gather.5.cloned.1.call-done = bf16[640,7168]{1,0:T(8,128)(2,1)} async-done(((bf16[40,7168]{1,0:T(8,128)(2,1)}), bf16[640,7168]{1,0:T(8,128)(2,1)}) %all-gather.5.cloned.1.call-update) | async-done | bytes 9175056 | tf_op jit(solution)/shard_map/all_gather | solution.py:52
  268.1 4.5 all-to-all-start.2
  272.9 7.0 %fusion.9 = f32[640,128]{0,1:T(8,128)S(1)} fusion(bf16[640,7168]{1,0:T(8,128)(2,1)} %all-gather.5.cloned.1.call-done, bf16[1,7168,128]{2,1,0:T(8,128)(2,1)} %param.10), kind=kOutput, calls=%fused_computation.27 | convolution fusion | flops 1174405120 | bytes 11337728 | tf_op jit(solution)/shard_map/dot_general | solution.py:62
  280.0 6.7 %fusion.2 = f32[640,128]{0,1:T(8,128)S(1)} fusion(bf16[640,7168]{1,0:T(8,128)(2,1)} %all-gather.7.cloned.1.call-done, bf16[1,128,7168]{2,1,0:T(8,128)(2,1)S(1)} %copy-done.2), kind=kOutput, calls=%fused_computation.7 | convolution fusion | flops 1174405120 | bytes 11337728 | tf_op jit(solution)/shard_map/dot_general | solution.py:67
  286.7 3.0 multiply_convert_fusion.2
  289.7 0.8 maximum_bitcast_fusion
  290.5 6.5 %convolution_convert_fusion = bf16[128,7168]{1,0:T(8,128)(2,1)} fusion(bf16[640,7168]{1,0:T(8,128)(2,1)} %all-gather.7.cloned.1.call-done, f32[640,128]{0,1:T(8,128)S(1)} %fusion.9, f32[640,128]{0,1:T(8,128)S(1)} %get-tuple-element.16), kind=kOutput, calls=%fused_computation | convolution fusion | flops 1175814144 | bytes 11665408 | tf_op jit(solution)/shard_map/dot_general | solution.py:73
  296.9 44.8 %all-to-all-done.2 = bf16[16,448,256]{2,1,0:T(8,128)(2,1)} async-done(((bf16[16,448,256]{2,1,0:T(8,128)(2,1)}), bf16[16,448,256]{2,1,0:T(8,128)(2,1)}, u32[]{:S(2)}, u32[]{:S(2)}) %all-to-all-start.2) | async-done | bytes 3670048 | tf_op jit(solution)/shard_map/all_to_all | solution.py:56
  341.7 2.8 collective-permute-start
  344.5 91.1 %all-gather.9.cloned.1.call-done = bf16[4096,640]{1,0:T(8,128)(2,1)} async-done(((bf16[256,640]{1,0:T(8,128)(2,1)}), bf16[4096,640]{1,0:T(8,128)(2,1)}) %all-gather.9.cloned.1.call-update) | async-done | bytes 5242896 | tf_op jit(solution)/shard_map/all_gather | solution.py:77
  435.7 6.6 %fusion.5 = bf16[640,448]{0,1:T(8,128)(2,1)S(1)} fusion(bf16[16,448,256]{2,1,0:T(8,128)(2,1)} %all-to-all-done.2, bf16[16,256,640]{2,1,0:T(8,128)(2,1)} %bitcast.68), kind=kOutput, calls=%fused_computation.11 | convolution fusion | flops 2349096960 | bytes 9486336 | tf_op jit(solution)/shard_map/dot_general | solution.py:78
  442.3 0.2 copy.29
  442.5 0.3 convert_element_type.54
  442.8 0.4 copy.30
  443.3 0.4 copy.31
  443.6 28.7 %all_to_all.22 = bf16[128,5,448]{2,1,0:T(8,128)(2,1)S(1)} all-to-all(bf16[128,5,448]{2,1,0:T(8,128)(2,1)S(1)} %copy.31), channel_id=1, replica_groups=mesh['pipe'=2,'group'=8,'member'=16] {'group','member'}, dimensions={0} | all-to-all | bytes 1146880 | tf_op jit(solution)/shard_map/all_to_all | solution.py:86
  472.6 0.8 reshape.117
  473.3 12.4 %collective-permute-start.2 = (bf16[40,7168]{1,0:T(8,128)(2,1)S(1)}, bf16[40,7168]{1,0:T(8,128)(2,1)S(1)}, u32[]{:S(2)}, u32[]{:S(2)}) collective-permute-start(bf16[40,7168]{1,0:T(8,128)(2,1)S(1)} %reshape.117), channel_id=1, source_target_pairs={{0,128},{128,0},{1,129},{129,1},{2,130},{130,2},{3,131},{131,3},{4... | collective-permute-start | bytes 1720328 | tf_op jit(solution)/shard_map/ppermute | solution.py:15
  486.0 1.3 collective-permute-done.1
  487.3 3.4 fusion.1
  (39 shorter events, 1.5 us)
Async XLA Ops:
  7.2 32.9 %copy-start = (bf16[1,128,7168]{2,1,0:T(8,128)(2,1)S(1)}, bf16[1,128,7168]{2,1,0:T(8,128)(2,1)}, u32[]{:S(2)}) copy-start(bf16[1,128,7168]{2,1,0:T(8,128)(2,1)} %param.7) | copy-start | bytes 5505028
  7.2 151.5 %all-gather.7.cloned.1.call-start = ((), (), s32[]{:S(2)}) async-start(), calls=%async_computation.5 | async-start | bytes 9748480 | tf_op jit(solution)/shard_map/all_gather | solution.py:53
  40.0 228.1 %all-gather.5.cloned.1.call-start = ((), (), s32[]{:S(2)}) async-start(), calls=%async_computation.4 | async-start | bytes 9748480 | tf_op jit(solution)/shard_map/all_gather | solution.py:52
  268.1 73.6 %all-to-all-start.2 = ((bf16[16,448,256]{2,1,0:T(8,128)(2,1)}), bf16[16,448,256]{2,1,0:T(8,128)(2,1)}, u32[]{:S(2)}, u32[]{:S(2)}) async-start(bf16[16,448,256]{2,1,0:T(8,128)(2,1)} %bitcast.56), calls=%async_computation.2 | async-start | bytes 7340032 | tf_op jit(solution)/shard_map/all_to_all | solution.py:56
  272.6 163.0 %all-gather.9.cloned.1.call-start = ((), (), s32[]{:S(2)}) async-start(), calls=%async_computation.6 | async-start | bytes 5570560 | tf_op jit(solution)/shard_map/all_gather | solution.py:77
  272.9 7.1 %copy-start.2 = (bf16[1,128,7168]{2,1,0:T(8,128)(2,1)S(1)}, bf16[1,128,7168]{2,1,0:T(8,128)(2,1)}, u32[]{:S(2)}) copy-start(bf16[1,128,7168]{2,1,0:T(8,128)(2,1)} %param.11) | copy-start | bytes 5505028
  272.9 13.8 %slice-start = ((s8[9175040]{0:T(1024)(128)(4,1)}), s8[4194304]{0:T(1024)(128)(4,1)S(1)}, s32[]{:S(2)}) async-start(s8[9175040]{0:T(1024)(128)(4,1)} %bitcast.54), calls=%async_computation.7 | async-start | bytes 8388608
  272.9 13.8 %slice-start.1 = ((s8[9175040]{0:T(1024)(128)(4,1)}), s8[4194304]{0:T(1024)(128)(4,1)S(1)}, s32[]{:S(2)}) async-start(s8[9175040]{0:T(1024)(128)(4,1)} %bitcast.54), calls=%async_computation.8 | async-start | bytes 8388608
  280.0 6.7 %slice-start.2 = ((s8[9175040]{0:T(1024)(128)(4,1)}), s8[786432]{0:T(1024)(128)(4,1)S(1)}, s32[]{:S(2)}) async-start(s8[9175040]{0:T(1024)(128)(4,1)} %bitcast.54), calls=%async_computation.9 | async-start | bytes 1572864
  280.0 6.7 %copy-start.1 = (bf16[1,7168,128]{2,1,0:T(8,128)(2,1)S(1)}, bf16[1,7168,128]{2,1,0:T(8,128)(2,1)}, u32[]{:S(2)}) copy-start(bf16[1,7168,128]{2,1,0:T(8,128)(2,1)} %param.9) | copy-start | bytes 5505028
  341.7 145.6 %collective-permute-start = (bf16[128,7168]{1,0:T(8,128)(2,1)}, bf16[128,7168]{1,0:T(8,128)(2,1)}, u32[]{:S(2)}, u32[]{:S(2)}) collective-permute-start(bf16[128,7168]{1,0:T(8,128)(2,1)} %bitcast.63), channel_id=1, source_target_pairs={{0,128},{128,0},{1,129},{129,1},{2,130},{130,2},{3,131},{131,3},{4... | collective-permute-start | bytes 5505032 | tf_op jit(solution)/shard_map/ppermute | solution.py:15
  473.3 14.0 %collective-permute-start.2 = (bf16[40,7168]{1,0:T(8,128)(2,1)S(1)}, bf16[40,7168]{1,0:T(8,128)(2,1)S(1)}, u32[]{:S(2)}, u32[]{:S(2)}) collective-permute-start(bf16[40,7168]{1,0:T(8,128)(2,1)S(1)} %reshape.117), channel_id=1, source_target_pairs={{0,128},{128,0},{1,129},{129,1},{2,130},{130,2},{3,131},{131,3},{4... | collective-permute-start | bytes 1720328 | tf_op jit(solution)/shard_map/ppermute | solution.py:15
  485.9 1.4 collective-permute-start.1
Sparse Core Ops, SparseCore 0:
  40.2 118.4 all-gather.6
  161.0 107.0 all-gather.4
  341.9 93.7 all-gather.8
where the time goes:
time: 498 us; the launch traced here: 497 us
  waiting for transfers between devices  343 us (69%)
  blocking collectives  69.4 us (14%)
  matrix products  35.4 us (7%)
  starting transfers between devices  20 us (4%)
  between operations  14 us (3%)
  local copies, waits for them, and re-layouts  8.14 us (2%)
  other arithmetic  7.01 us (1%)
    all_gather x1, waiting for transfers between devices, body(): got_in = lax.all_gather(near_in, 'member', axis=0, tiled=True)  109 us
    all_gather x1, waiting for transfers between devices, body(): got_grad = lax.all_gather(near_grad, 'member', axis=0, tiled=True)  96.5 us
    all_gather x1, waiting for transfers between devices, body(): all_grad = lax.all_gather(both_grad, 'member', axis=0, tiled=False)  91.1 us
    all_to_all x1, waiting for transfers between devices, body(): lax.all_to_all(both_cols.reshape(SHARDS, -1, both_cols.shape[1]), 'member...  44.8 us
    all_to_all x1, blocking collectives, body(): lax.all_to_all(slice_value.astype(jnp.bfloat16), ('group', 'member'), 0,...  28.7 us
    all_to_all x1, blocking collectives, body(): lax.all_to_all(send_grad, 'group', 0, 0, tiled=True)  26.1 us
    ppermute x3, starting transfers between devices, from_behind(): return lax.ppermute(value, axis, pairs)  15.2 us
    all_to_all x1, blocking collectives, body(): lax.all_to_all(send_in, 'group', 0, 0, tiled=True)  14.6 us
  transfers between devices with their start and end apart: 7, of which 5 were waited for; matrix products, arithmetic and copies ran while one was open for 8% of the time, Pallas kernels for 0%

commit v1 on v0

--- a/solution.py
+++ b/solution.py
@@ -49,7 +49,9 @@
     near_rows = live_count * slot_count
     near_in = lax.all_to_all(send_in, "group", 0, 0, tiled=True).reshape(near_rows, model_width)
     near_grad = lax.all_to_all(send_grad, "group", 0, 0, tiled=True).reshape(near_rows, model_width)
-    got_in = lax.all_gather(near_in, "member", axis=0, tiled=True)
+    got_in = jnp.concatenate(
+        lax.all_to_all(jnp.stack([near_in] * lax.axis_size("member")), "member", 0, 0), axis=0
+    )
     got_grad = lax.all_gather(near_grad, "member", axis=0, tiled=True)
     both_cols = jnp.concatenate([gate_cols, up_cols], axis=1)
     both_cols, got_in, got_grad = lax.optimization_barrier((both_cols, got_in, got_grad))

time: 498 us -> 595 us (1.19)
  waiting for transfers between devices: 343 us -> 411 us
  starting transfers between devices: 20 us -> 85.7 us
  blocking collectives: 69.4 us -> 28.7 us
    all_gather x1, waiting for transfers between devices: 96.5 us -> 220 us  [body(): got_grad = lax.all_gather(near_grad, 'member', axis=0, tiled=True)]
    all_gather x1 -> x0, waiting for transfers between devices: 109 us -> none  [body(): got_in = lax.all_gather(near_in, 'member', axis=0, tiled=True)]
    all_to_all x0 -> x3, waiting for transfers between devices: none -> 50.9 us  [the longest x1 27.8 us: body(): lax.all_to_all(jnp.stack([near_in] * lax.axis_size('member')), 'member',...]
    all_to_all x2 -> x0, blocking collectives: 40.7 us -> none  [the longest x1 26.1 us: body(): lax.all_to_all(send_grad, 'group', 0, 0, tiled=True)]
    all_to_all x1, starting transfers between devices: 4.52 us -> 39.5 us  [body(): lax.all_to_all(both_cols.reshape(SHARDS, -1, both_cols.shape[1]), 'member...]
    all_to_all x0 -> x3, starting transfers between devices: none -> 30.7 us  [the longest x1 15.6 us: body(): lax.all_to_all(jnp.stack([near_in] * lax.axis_size('member')), 'member',...]
  transfers between devices with their start and end apart: 7 -> 9, of which waited for: 5 -> 7; matrix products, arithmetic and copies ran while one was open for 8% -> 8% of each run, Pallas kernels for 0% -> 0%
where the time goes in v1:
time: 595 us
  waiting for transfers between devices  411 us (69%)
  starting transfers between devices  85.7 us (14%)
  matrix products  34.7 us (6%)
  blocking collectives  28.7 us (5%)
  between operations  14.2 us (2%)
  local copies, waits for them, and re-layouts  13.8 us (2%)
  other arithmetic  6.51 us (1%)
    all_gather x1, waiting for transfers between devices, body(): got_grad = lax.all_gather(near_grad, 'member', axis=0, tiled=True)  220 us
    all_gather x1, waiting for transfers between devices, body(): all_grad = lax.all_gather(both_grad, 'member', axis=0, tiled=False)  93.8 us
    all_to_all x1, waiting for transfers between devices, body(): lax.all_to_all(both_cols.reshape(SHARDS, -1, both_cols.shape[1]), 'member...  45.5 us
    all_to_all x1, starting transfers between devices, body(): lax.all_to_all(both_cols.reshape(SHARDS, -1, both_cols.shape[1]), 'member...  39.5 us
    all_to_all x1, blocking collectives, body(): lax.all_to_all(slice_value.astype(jnp.bfloat16), ('group', 'member'), 0,...  28.7 us
    all_to_all x1, waiting for transfers between devices, body(): lax.all_to_all(jnp.stack([near_in] * lax.axis_size('member')), 'member',...  27.8 us
    all_to_all x1, starting transfers between devices, body(): lax.all_to_all(jnp.stack([near_in] * lax.axis_size('member')), 'member',...  15.6 us
    ppermute x3, starting transfers between devices, from_behind(): return lax.ppermute(value, axis, pairs)  15.3 us
  transfers between devices with their start and end apart: 9, of which 7 were waited for; matrix products, arithmetic and copies ran while one was open for 8% of the time, Pallas kernels for 0%

profile of v1, /device:TPU:1, one launch (start us, length us, event | category | flops | bytes accessed | tf_op | source)
XLA Modules:
  0.0 594.9 jit_solution(7887377844739609826)
XLA Ops:
  7.2 0.8 convert_reduce_fusion
  8.4 0.7 select_reduce_fusion.1
  9.3 1.9 fusion
  11.2 1.8 reshape.115
  13.0 11.5 %all-to-all-start.2 = ((bf16[8,16,2240]{2,1,0:T(8,128)(2,1)}), bf16[8,16,2240]{2,1,0:T(8,128)(2,1)S(1)}, u32[]{:S(2)}, u32[]{:S(2)}) async-start(bf16[8,16,2240]{2,1,0:T(8,128)(2,1)} %reshape.115), calls=%async_computation.2 | async-start | bytes 1179648 | tf_op jit(solution)/shard_map/all_to_all | solution.py:51
  24.9 1.8 reshape.113
  26.6 12.7 %all-to-all-done.2 = bf16[8,16,2240]{2,1,0:T(8,128)(2,1)S(1)} async-done(((bf16[8,16,2240]{2,1,0:T(8,128)(2,1)}), bf16[8,16,2240]{2,1,0:T(8,128)(2,1)S(1)}, u32[]{:S(2)}, u32[]{:S(2)}) %all-to-all-start.2) | async-done | bytes 573472 | tf_op jit(solution)/shard_map/all_to_all | solution.py:51
  39.3 3.5 all-to-all-start
  42.9 1.7 reshape.116
  44.7 10.4 %all-to-all-done = bf16[8,16,2240]{2,1,0:T(8,128)(2,1)S(1)} async-done(((bf16[8,16,2240]{2,1,0:T(8,128)(2,1)}), bf16[8,16,2240]{2,1,0:T(8,128)(2,1)S(1)}, u32[]{:S(2)}, u32[]{:S(2)}) %all-to-all-start) | async-done | bytes 573472 | tf_op jit(solution)/shard_map/all_to_all | solution.py:50
  55.1 0.9 stack_reshape.2
  56.0 4.7 stack.3
  60.8 15.6 %all-to-all-start.1 = ((bf16[16,40,7168]{2,1,0:T(8,128)(2,1)}), bf16[16,40,7168]{2,1,0:T(8,128)(2,1)}, u32[]{:S(2)}, u32[]{:S(2)}) async-start(bf16[16,40,7168]{2,1,0:T(8,128)(2,1)} %stack.3), calls=%async_computation.1 | async-start | bytes 18350080 | tf_op jit(solution)/shard_map/all_to_all | solution.py:53
  76.4 3.8 pad_maximum_fusion
  80.2 219.6 %all-gather.4.cloned.1.call-done = bf16[640,7168]{1,0:T(8,128)(2,1)} async-done(((bf16[40,7168]{1,0:T(8,128)(2,1)}), bf16[640,7168]{1,0:T(8,128)(2,1)}) %all-gather.4.cloned.1.call-update) | async-done | bytes 9175056 | tf_op jit(solution)/shard_map/all_gather | solution.py:55
  299.9 27.8 %all-to-all-done.1 = bf16[16,40,7168]{2,1,0:T(8,128)(2,1)} async-done(((bf16[16,40,7168]{2,1,0:T(8,128)(2,1)}), bf16[16,40,7168]{2,1,0:T(8,128)(2,1)}, u32[]{:S(2)}, u32[]{:S(2)}) %all-to-all-start.1) | async-done | bytes 9175072 | tf_op jit(solution)/shard_map/all_to_all | solution.py:53
  327.6 39.5 %all-to-all-start.3 = ((bf16[16,448,256]{2,1,0:T(8,128)(2,1)}), bf16[16,448,256]{2,1,0:T(8,128)(2,1)}, u32[]{:S(2)}, u32[]{:S(2)}) async-start(bf16[16,448,256]{2,1,0:T(8,128)(2,1)} %bitcast.55), calls=%async_computation.3 | async-start | bytes 7340032 | tf_op jit(solution)/shard_map/all_to_all | solution.py:58
  367.4 6.5 %fusion.9 = f32[640,128]{0,1:T(8,128)S(1)} fusion(bf16[640,7168]{1,0:T(8,128)(2,1)} %bitcast.5, bf16[1,7168,128]{2,1,0:T(8,128)(2,1)S(1)} %copy-done.3), kind=kOutput, calls=%fused_computation.27 | convolution fusion | flops 1174405120 | bytes 11337728 | tf_op jit(solution)/shard_map/dot_general | solution.py:64
  374.1 2.9 fusion.2
  377.0 6.5 %multiply_convert_fusion.2 = (bf16[640,128]{0,1:T(8,128)(2,1)S(1)}, bf16[640,128]{0,1:T(8,128)(2,1)S(1)}, f32[640,128]{0,1:T(8,128)S(1)}) fusion(f32[640,128]{0,1:T(8,128)S(1)} %fusion.2, f32[640,128]{0,1:T(8,128)S(1)} %fusion.9, bf16[640,7168]{1,0:T(8,128)(2,1)} %bitcast.5, bf16[1,7168,128]{2,1,0:T(8,128)(2,1)S(1)} %copy-done.4), kind=kOutput, calls=%fused_computation.16 | convolution fusion | flops 1175470080 | bytes 12320768 | tf_op jit(solution)/shard_map/dot_general | solution.py:63
  383.5 0.8 maximum_bitcast_fusion
  384.3 6.5 %convolution_convert_fusion = bf16[128,7168]{1,0:T(8,128)(2,1)} fusion(bf16[640,7168]{1,0:T(8,128)(2,1)} %all-gather.4.cloned.1.call-done, f32[640,128]{0,1:T(8,128)S(1)} %fusion.9, f32[640,128]{0,1:T(8,128)S(1)} %get-tuple-element.16), kind=kOutput, calls=%fused_computation | convolution fusion | flops 1175814144 | bytes 11665408 | tf_op jit(solution)/shard_map/dot_general | solution.py:75
  390.7 45.5 %all-to-all-done.3 = bf16[16,448,256]{2,1,0:T(8,128)(2,1)} async-done(((bf16[16,448,256]{2,1,0:T(8,128)(2,1)}), bf16[16,448,256]{2,1,0:T(8,128)(2,1)}, u32[]{:S(2)}, u32[]{:S(2)}) %all-to-all-start.3) | async-done | bytes 3670048 | tf_op jit(solution)/shard_map/all_to_all | solution.py:58
  436.3 2.8 collective-permute-start
  439.1 93.8 %all-gather.6.cloned.1.call-done = bf16[4096,640]{1,0:T(8,128)(2,1)} async-done(((bf16[256,640]{1,0:T(8,128)(2,1)}), bf16[4096,640]{1,0:T(8,128)(2,1)}) %all-gather.6.cloned.1.call-update) | async-done | bytes 5242896 | tf_op jit(solution)/shard_map/all_gather | solution.py:79
  532.9 6.6 %fusion.5 = bf16[640,448]{0,1:T(8,128)(2,1)S(1)} fusion(bf16[16,448,256]{2,1,0:T(8,128)(2,1)} %all-to-all-done.3, bf16[16,256,640]{2,1,0:T(8,128)(2,1)} %bitcast.66), kind=kOutput, calls=%fused_computation.11 | convolution fusion | flops 2349096960 | bytes 9486336 | tf_op jit(solution)/shard_map/dot_general | solution.py:80
  540.1 0.4 copy.30
  540.9 28.7 %all_to_all.25 = bf16[128,5,448]{2,1,0:T(8,128)(2,1)S(1)} all-to-all(bf16[128,5,448]{2,1,0:T(8,128)(2,1)S(1)} %copy.31), channel_id=1, replica_groups=mesh['pipe'=2,'group'=8,'member'=16] {'group','member'}, dimensions={0} | all-to-all | bytes 1146880 | tf_op jit(solution)/shard_map/all_to_all | solution.py:88
  569.9 0.8 reshape.119
  570.6 12.4 %collective-permute-start.2 = (bf16[40,7168]{1,0:T(8,128)(2,1)S(1)}, bf16[40,7168]{1,0:T(8,128)(2,1)S(1)}, u32[]{:S(2)}, u32[]{:S(2)}) collective-permute-start(bf16[40,7168]{1,0:T(8,128)(2,1)S(1)} %reshape.119), channel_id=1, source_target_pairs={{0,128},{128,0},{1,129},{129,1},{2,130},{130,2},{3,131},{131,3},{4... | collective-permute-start | bytes 1720328 | tf_op jit(solution)/shard_map/ppermute | solution.py:15
  583.3 1.3 collective-permute-done.1
  584.6 3.4 fusion.1
  (40 shorter events, 2.8 us)
Async XLA Ops:
  7.2 17.3 %copy-start = (bf16[1,128,7168]{2,1,0:T(8,128)(2,1)S(1)}, bf16[1,128,7168]{2,1,0:T(8,128)(2,1)}, u32[]{:S(2)}) copy-start(bf16[1,128,7168]{2,1,0:T(8,128)(2,1)} %param.7) | copy-start | bytes 5505028
  13.0 26.4 %all-to-all-start.2 = ((bf16[8,16,2240]{2,1,0:T(8,128)(2,1)}), bf16[8,16,2240]{2,1,0:T(8,128)(2,1)S(1)}, u32[]{:S(2)}, u32[]{:S(2)}) async-start(bf16[8,16,2240]{2,1,0:T(8,128)(2,1)} %reshape.115), calls=%async_computation.2 | async-start | bytes 1179648 | tf_op jit(solution)/shard_map/all_to_all | solution.py:51
  39.3 15.8 %all-to-all-start = ((bf16[8,16,2240]{2,1,0:T(8,128)(2,1)}), bf16[8,16,2240]{2,1,0:T(8,128)(2,1)S(1)}, u32[]{:S(2)}, u32[]{:S(2)}) async-start(bf16[8,16,2240]{2,1,0:T(8,128)(2,1)} %reshape.113), calls=%async_computation | async-start | bytes 1179648 | tf_op jit(solution)/shard_map/all_to_all | solution.py:50
  42.9 257.0 %all-gather.4.cloned.1.call-start = ((), (), s32[]{:S(2)}) async-start(), calls=%async_computation.5 | async-start | bytes 9748480 | tf_op jit(solution)/shard_map/all_gather | solution.py:55
  60.8 15.7 %copy-start.3 = (bf16[1,7168,128]{2,1,0:T(8,128)(2,1)S(1)}, bf16[1,7168,128]{2,1,0:T(8,128)(2,1)}, u32[]{:S(2)}) copy-start(bf16[1,7168,128]{2,1,0:T(8,128)(2,1)} %param.10) | copy-start | bytes 5505028
  60.8 266.9 %all-to-all-start.1 = ((bf16[16,40,7168]{2,1,0:T(8,128)(2,1)}), bf16[16,40,7168]{2,1,0:T(8,128)(2,1)}, u32[]{:S(2)}, u32[]{:S(2)}) async-start(bf16[16,40,7168]{2,1,0:T(8,128)(2,1)} %stack.3), calls=%async_computation.1 | async-start | bytes 18350080 | tf_op jit(solution)/shard_map/all_to_all | solution.py:53
  327.6 108.6 %all-to-all-start.3 = ((bf16[16,448,256]{2,1,0:T(8,128)(2,1)}), bf16[16,448,256]{2,1,0:T(8,128)(2,1)}, u32[]{:S(2)}, u32[]{:S(2)}) async-start(bf16[16,448,256]{2,1,0:T(8,128)(2,1)} %bitcast.55), calls=%async_computation.3 | async-start | bytes 7340032 | tf_op jit(solution)/shard_map/all_to_all | solution.py:58
  367.1 165.8 %all-gather.6.cloned.1.call-start = ((), (), s32[]{:S(2)}) async-start(), calls=%async_computation.6 | async-start | bytes 5570560 | tf_op jit(solution)/shard_map/all_gather | solution.py:79
  367.4 6.6 %copy-start.2 = (bf16[640,7168]{1,0:T(8,128)(2,1)S(1)}, bf16[640,7168]{1,0:T(8,128)(2,1)}, u32[]{:S(2)}) copy-start(bf16[640,7168]{1,0:T(8,128)(2,1)} %all-gather.4.cloned.1.call-done) | copy-start | bytes 27525124
  367.4 6.7 %copy-start.5 = (bf16[1,128,7168]{2,1,0:T(8,128)(2,1)S(1)}, bf16[1,128,7168]{2,1,0:T(8,128)(2,1)}, u32[]{:S(2)}) copy-start(bf16[1,128,7168]{2,1,0:T(8,128)(2,1)} %param.11) | copy-start | bytes 5505028
  374.1 3.0 copy-start.4
  436.3 148.3 %collective-permute-start = (bf16[128,7168]{1,0:T(8,128)(2,1)}, bf16[128,7168]{1,0:T(8,128)(2,1)}, u32[]{:S(2)}, u32[]{:S(2)}) collective-permute-start(bf16[128,7168]{1,0:T(8,128)(2,1)} %bitcast), channel_id=1, source_target_pairs={{0,128},{128,0},{1,129},{129,1},{2,130},{130,2},{3,131},{131,3},{4... | collective-permute-start | bytes 5505032 | tf_op jit(solution)/shard_map/ppermute | solution.py:15
  569.6 18.4 %copy-start.1 = (bf16[1,128,7168]{2,1,0:T(8,128)(2,1)S(1)}, bf16[1,128,7168]{2,1,0:T(8,128)(2,1)}, u32[]{:S(2)}) copy-start(bf16[1,128,7168]{2,1,0:T(8,128)(2,1)} %param.7) | copy-start | bytes 5505028
  570.6 14.0 %collective-permute-start.2 = (bf16[40,7168]{1,0:T(8,128)(2,1)S(1)}, bf16[40,7168]{1,0:T(8,128)(2,1)S(1)}, u32[]{:S(2)}, u32[]{:S(2)}) collective-permute-start(bf16[40,7168]{1,0:T(8,128)(2,1)S(1)} %reshape.119), channel_id=1, source_target_pairs={{0,128},{128,0},{1,129},{129,1},{2,130},{130,2},{3,131},{131,3},{4... | collective-permute-start | bytes 1720328 | tf_op jit(solution)/shard_map/ppermute | solution.py:15
  583.2 1.4 collective-permute-start.1
Sparse Core Ops, SparseCore 0:
  46.1 253.7 all-gather.3
  436.4 96.4 all-gather.5
